TPU v7x, 32 devices: a whole 2x2x4 slice. The times are simulated.
32 devices in a mesh: row: 4 (over y, x), col: 8 (over z, core).
Axes of the slice: x: 2, y: 2, z: 4, core: 2. Of those that a mesh axis runs over, the one named last changes fastest.
Arguments:
- covariance: float32 [20, 4, 10, 8, 256, 256], P(None, 'row', None, 'col'), may hold values from -0.006 to 2.4, as said below
- telemetry: bfloat16 [1536, 10, 8, 256], P('row', None, 'col'), may hold values from -6 to 6
- active: int32 [8, 1280], replicated, may hold values 0 or 1
- panel: int32 [1], replicated, may hold values from 0 to 75
Outputs:
- factored: float32 [20, 4, 10, 8, 256, 256], P(None, 'row', None, 'col')
Inputs may be any that keep to these rules, and one draw needn't show every extreme that they name: `covariance`: in every diagonal tile each diagonal entry exceeds the sum of magnitudes of the other entries of its row; entries off the matrix diagonal lie in -0.006 to 0.006.
All inputs are finite; a program needn't handle non-finite values.
Results may differ from a plain program's by a relative error of at most 0.0006.
Values may be sent and summed in bfloat16 or wider, within the bound.
No kernel may reach another device: no remote copies, remote signals or barrier semaphores. Data moves between devices by JAX's collectives and lax.ppermute only.
A program may use at most 384 MiB of HBM per device.

v0:
```python
import jax
import jax.numpy as jnp
from jax import lax
from jax.sharding import PartitionSpec as P

FORGET = 0.9


def from_root(block, axis, holder):
    block = jnp.where(lax.axis_index(axis) == holder, block, jnp.zeros_like(block))
    return lax.psum(block, axis)


def body(covariance, telemetry, active, panel):
    n_row = lax.axis_size("row")
    n_col = lax.axis_size("col")
    row_index = lax.axis_index("row")
    col_index = lax.axis_index("col")
    blocks_a = covariance.shape[0]
    blocks_b = covariance.shape[2]
    width = covariance.shape[4]
    ratio = n_col // n_row
    samples = telemetry.shape[0] * n_row
    tiles = blocks_b * n_col
    earlier = covariance[:, 0, :, 0]
    local = telemetry[:, :, 0, :]
    mask_full = jnp.concatenate([active, active], axis=1).reshape(tiles, width).astype(jnp.bfloat16)
    col_mask = lax.dynamic_index_in_dim(
        mask_full.reshape(blocks_b, n_col, width), col_index, 1, keepdims=False
    )
    row_mask = lax.dynamic_index_in_dim(
        mask_full.reshape(blocks_a, n_row, width), row_index, 1, keepdims=False
    )
    column_data = lax.all_gather(local, "row", axis=0, tiled=True)
    slabs = []
    for offset in range(ratio):
        slabs.append(from_root(column_data, "col", row_index + offset * n_row))
    row_data = jnp.stack(slabs, axis=2).reshape(samples, blocks_a, width)
    column_data = column_data * col_mask[None]
    row_data = row_data * row_mask[None]
    row_tiles = jnp.arange(blocks_a, dtype=jnp.int32) * n_row + row_index
    col_tiles = jnp.arange(blocks_b, dtype=jnp.int32) * n_col + col_index
    lower = row_tiles[:, None] >= col_tiles[None, :]
    gram = jnp.einsum("sat,sbu->abtu", row_data, column_data, preferred_element_type=jnp.float32)
    fresh = jnp.where(lower[:, :, None, None], FORGET * earlier + gram / samples, earlier)
    panel_at = panel[0]
    owner_row = panel_at % n_row
    owner_col = panel_at % n_col
    diag_tile = lax.dynamic_slice(
        fresh, (panel_at // n_row, panel_at // n_col, 0, 0), (1, 1, width, width)
    )[0, 0]
    factor = jnp.linalg.cholesky(diag_tile)
    inverse = lax.linalg.triangular_solve(
        factor, jnp.eye(width, dtype=jnp.float32), left_side=True, lower=True
    )
    inverse = from_root(inverse, "row", owner_row)
    column_part = lax.dynamic_index_in_dim(fresh, panel_at // n_col, 1, keepdims=False)
    solved = jnp.einsum(
        "atu,vu->atv",
        column_part,
        inverse,
        precision=lax.Precision.HIGHEST,
        preferred_element_type=jnp.float32,
    )
    solved = jnp.where((row_tiles > panel_at)[:, None, None], solved, jnp.zeros_like(solved))
    panel_rows = from_root(solved.astype(jnp.bfloat16), "col", owner_col).astype(solved.dtype)
    pick = col_index // n_row
    chosen = lax.dynamic_index_in_dim(
        panel_rows.reshape(blocks_b, ratio, width, width), pick, 1, keepdims=False
    )
    panel_cols = from_root(chosen.astype(jnp.bfloat16), "row", col_index % n_row).astype(
        chosen.dtype
    )
    trailing = lower & (col_tiles[None, :] > panel_at)
    update = jnp.einsum(
        "atv,buv->abtu",
        panel_rows,
        panel_cols,
        precision=lax.Precision.HIGHEST,
        preferred_element_type=jnp.float32,
    )
    result = jnp.where(trailing[:, :, None, None], fresh - update, fresh)
    on_column = (col_tiles == panel_at)[None, :] & (row_tiles > panel_at)[:, None]
    result = jnp.where(on_column[:, :, None, None], panel_rows[:, None], result)
    on_diagonal = (col_tiles == panel_at)[None, :] & (row_tiles == panel_at)[:, None]
    result = jnp.where(on_diagonal[:, :, None, None], factor[None, None], result)
    return result[:, None, :, None]


def solution(mesh):
    in_specs = (P(None, "row", None, "col", None, None), P("row", None, "col", None), P(), P())
    out_specs = P(None, "row", None, "col", None, None)
    return jax.shard_map(body, mesh=mesh, in_specs=in_specs, out_specs=out_specs, check_vma=False)
```

profile of v0, /device:TPU:0, one launch (start us, length us, event | category | flops | bytes accessed | tf_op | source)
XLA Modules:
  0.0 831.1 jit_solution(5645800348601662963)
XLA Ops:
  7.3 87.7 %all-gather.3.cloned.1.call-done = bf16[1536,10,1,256]{3,0,1,2:T(8,128)(2,1)} async-done(((bf16[384,10,1,256]{3,0,1,2:T(8,128)(2,1)}), bf16[1536,10,1,256]{3,0,1,2:T(8,128)(2,1)}) %all-gather.3.cloned.1.call-update) | async-done | bytes 7864336 | tf_op jit(solution)/shard_map/all_gather | solution.py:34
  95.0 9.7 %fusion.6 = (bf16[1536,10,1,256]{3,0,1,2:T(8,128)(2,1)}, bf16[1536,10,1,256]{3,0,2,1:T(8,128)(2,1)}) fusion(bf16[1536,10,1,256]{3,0,1,2:T(8,128)(2,1)} %all-gather.3.cloned.1.call-done, pred[]{:T(512)S(6)} %eq.50, pred[]{:T(512)S(6)} %eq.51), kind=kLoop, calls=%fused_computation.16 | loop fusion | flops 7864320 | bytes 23592962 | tf_op jit(solution)/shard_map/stack | solution.py:38
  105.8 49.6 %copy.22 = f32[20,1,10,1,256,256]{4,5,0,2,3,1:T(8,128)} copy(f32[20,1,10,1,256,256]{5,4,3,2,1,0:T(8,128)} %param.4) | data formatting | bytes 104857600 | tf_op args[0]
  155.6 263.2 %all-reduce.13.cloned.1.call-done = (bf16[1536,10,1,256]{3,0,2,1:T(8,128)(2,1)}, bf16[1536,10,1,256]{3,0,1,2:T(8,128)(2,1)}) async-done(((bf16[1536,10,1,256]{3,0,2,1:T(8,128)(2,1)}, bf16[1536,10,1,256]{3,0,1,2:T(8,128)(2,1)}), (bf16[1536,10,1,256]{3,0,2,1:T(8,128)(2,1)}, bf16[1536,10,1,256]{3,0,1,2:T(8,128)(2,1)})) %all-reduce.13.cloned.1.call-update) | async-done | bytes 15728656 | tf_op jit(solution)/shard_map/psum | solution.py:11
  418.8 7.8 pad_maximum_fusion
  426.6 6.5 bitcast_multiply_fusion.1
  433.1 56.1 %fusion.3 = f32[20,10,256,256]{2,3,0,1:T(8,128)} fusion(f32[20,1,10,1,256,256]{4,5,0,2,3,1:T(8,128)} %copy.22, pred[20,10]{0,1:T(8,128)(4,1)S(1)} %get-tuple-element.34, bf16[1536,20,256]{2,0,1:T(8,128)(2,1)} %bitcast_multiply_fusion.1, bf16[1536,10,1,256]{3,0,1,2:T(8,128)(2,1)} %all-gather.3.cloned.1.call-done, bf16[10,256]{1,0:T(8,128)(2,1)S(1)} %bitcast.126), kind=kOutput, calls=%fused_computation.7 | convolution fusion | flops 40333475840 | bytes 128455880 | tf_op jit(solution)/shard_map/sat,sbu->abtu/dot_general | solution.py:44
  489.2 1.0 dynamic-slice_bitcast_fusion
  490.3 1.0 fusion.19
  491.3 11.7 %cholesky.50 = f32[128,128]{1,0:T(8,128)S(1)} custom-call(f32[128,128]{1,0:T(8,128)S(1)} %cholesky.118), custom_call_target="Cholesky" | custom-call | tf_op jit(solution)/shard_map/jit(cholesky)/cholesky | solution.py:52
  503.1 9.8 %custom-call.14 = f32[1,128,128]{1,2,0:T(8,128)S(1)} custom-call(f32[1,128,128]{2,1,0:T(8,128)S(1)} %get-tuple-element.32), custom_call_target="InvertDiagBlocksLowerTriangular" | custom-call | tf_op jit(solution)/shard_map/jit(cholesky)/cholesky | solution.py:52
  513.4 11.7 %cholesky.105 = f32[128,128]{1,0:T(8,128)S(1)} custom-call(f32[128,128]{1,0:T(8,128)S(1)} %convolution_subtract_fusion.1), custom_call_target="Cholesky" | custom-call | tf_op jit(solution)/shard_map/jit(cholesky)/cholesky | solution.py:52
  527.3 3.9 while.1
  527.9 1.3 bitcast_dynamic-update-slice_fusion.2
  529.8 1.3 bitcast_dynamic-update-slice_fusion.2
  531.2 19.9 %custom-call.15 = f32[2,128,128]{1,2,0:T(8,128)S(1)} custom-call(f32[2,128,128]{2,1,0:T(8,128)S(1)} %get-tuple-element.12), custom_call_target="InvertDiagBlocksLowerTriangular" | custom-call | tf_op jit(solution)/shard_map/triangular_solve | solution.py:53
  552.8 43.4 %all-reduce.7.cloned.1.call-done = f32[256,256]{1,0:T(8,128)} async-done(((f32[256,256]{1,0:T(8,128)}), f32[256,256]{1,0:T(8,128)}) %all-reduce.7.cloned.1.call-update) | async-done | bytes 262160 | tf_op jit(solution)/shard_map/psum | solution.py:11
  596.1 12.9 %fusion.12 = bf16[20,256,256]{2,1,0:T(8,128)(2,1)} fusion(pred[20]{0:T(512)(128)(4,1)S(1)} %broadcast_compare_fusion.1, pred[]{:T(512)S(6)} %eq.52, f32[20,10,256,256]{2,3,0,1:T(8,128)} %fusion.3, s32[]{:T(128)S(6)} %select_n.120, f32[256,256]{1,0:T(8,128)} %all-reduce.7.cloned.1.call-done), kind=kOutput, calls=%fused_computation.23 | convolution fusion | flops 4030464000 | bytes 8126489 | tf_op jit(solution)/shard_map/atu,vu->atv/dot_general | solution.py:58
  609.1 69.2 %all-reduce.9.cloned.1.call-done = bf16[20,256,256]{2,1,0:T(8,128)(2,1)} async-done(((bf16[20,256,256]{2,1,0:T(8,128)(2,1)}), bf16[20,256,256]{2,1,0:T(8,128)(2,1)}) %all-reduce.9.cloned.1.call-update) | async-done | bytes 2621456 | tf_op jit(solution)/shard_map/psum | solution.py:11
  678.3 2.6 fusion.17
  681.2 5.1 copy.29
  686.4 50.4 %all-reduce.11.cloned.1.call-done = bf16[10,256,256]{2,1,0:T(8,128)(2,1)} async-done(((bf16[10,256,256]{2,1,0:T(8,128)(2,1)}), bf16[10,256,256]{2,1,0:T(8,128)(2,1)}) %all-reduce.11.cloned.1.call-update) | async-done | bytes 1310736 | tf_op jit(solution)/shard_map/psum | solution.py:11
  736.8 35.7 %fusion.2 = f32[20,1,10,1,256,256]{4,5,0,2,3,1:T(8,128)} fusion(f32[20,10,256,256]{2,3,0,1:T(8,128)} %fusion.3, f32[20,256,256]{1,2,0:T(8,128)} %copy.29, f32[256,256]{0,1:T(8,128)S(1)} %copy.27, pred[20,10]{0,1:T(8,128)(4,1)S(1)} %get-tuple-element.33, pred[20,10]{0,1:T(8,128)(4,1)S(1)} %get-tuple-element.36, pred[20,10]{0,1:T(8,128)(4,1)S(1)} %get-tuple-element.35, ...), kind=kOutput, calls=%fused_computation.5 | convolution fusion | flops 6763315200 | bytes 114295384 | tf_op jit(solution)/shard_map/atv,buv->abtu/dot_general | solution.py:75
  772.4 52.2 %copy.31 = f32[20,1,10,1,256,256]{5,4,3,2,1,0:T(8,128)} copy(f32[20,1,10,1,256,256]{4,5,0,2,3,1:T(8,128)} %fusion.2) | data formatting | bytes 104857600 | tf_op jit(solution)/shard_map/broadcast_in_dim | solution.py:87
  (51 shorter events, 5.8 us)
Async XLA Ops:
  6.5 88.5 %all-gather.3.cloned.1.call-start = ((), (), s32[]{:S(2)}) async-start(), calls=%async_computation.3 | async-start | bytes 9830400 | tf_op jit(solution)/shard_map/all_gather | solution.py:34
  7.3 411.6 %all-reduce.13.cloned.1.call-start = ((), (), s32[]{:S(2)}) async-start(), calls=%async_computation.4 | async-start | bytes 31457280 | tf_op jit(solution)/shard_map/psum | solution.py:11
  104.8 0.8 copy-start.1
  104.8 491.3 %all-reduce.7.cloned.1.call-start = ((), (), s32[]{:S(2)}) async-start(), calls=%async_computation | async-start | bytes 524288 | tf_op jit(solution)/shard_map/psum | solution.py:11
  552.7 125.7 %all-reduce.9.cloned.1.call-start = ((), (), s32[]{:S(2)}) async-start(), calls=%async_computation.1 | async-start | bytes 5242880 | tf_op jit(solution)/shard_map/psum | solution.py:11
  609.1 127.7 %all-reduce.11.cloned.1.call-start = ((), (), s32[]{:S(2)}) async-start(), calls=%async_computation.2 | async-start | bytes 2621440 | tf_op jit(solution)/shard_map/psum | solution.py:11
  678.3 58.4 %copy-start = (bf16[20,256,256]{2,1,0:T(8,128)(2,1)S(1)}, bf16[20,256,256]{2,1,0:T(8,128)(2,1)}, u32[]{:S(2)}) copy-start(bf16[20,256,256]{2,1,0:T(8,128)(2,1)} %all-reduce.9.cloned.1.call-done) | copy-start | bytes 7864324
Sparse Core Ops, SparseCore 0:
  9.2 85.8 all-gather.2
  104.9 313.8 all-reduce.12
  552.8 43.3 all-reduce.6
  609.2 69.1 all-reduce.8
  681.3 55.4 all-reduce.10
where the time goes:
time: 833 us; the launch traced here: 831 us
  waiting for transfers between devices  515 us (62%)
  local copies, waits for them, and re-layouts  112 us (13%)
  matrix products  106 us (13%)
  other arithmetic  82.5 us (10%)
  between operations  15.4 us (2%)
    psum x4, waiting for transfers between devices, from_root(): return lax.psum(block, axis)  426 us
    all_gather x1, waiting for transfers between devices, body(): column_data = lax.all_gather(local, 'row', axis=0, tiled=True)  87.7 us
    dot_general x1, matrix products, body(): jnp.einsum('sat,sbu->abtu', row_data, column_data, preferred_element_type...  56.1 us
    broadcast_in_dim x1, local copies, waits for them, and re-layouts, body(): return result[:, None, :, None]  52.2 us
    unnamed x7, local copies, waits for them, and re-layouts  49.6 us
    dot_general x1, matrix products, body(): jnp.einsum('atv,buv->abtu', panel_rows, panel_cols, precision=lax.Precisi...  35.7 us
    another operation x6, other arithmetic, body(): factor = jnp.linalg.cholesky(diag_tile)  34 us
    another operation x3, other arithmetic, body(): lax.linalg.triangular_solve(factor, jnp.eye(width, dtype=jnp.float32), le...  19.9 us
  transfers between devices with their start and end apart: 5, of which 5 were waited for; matrix products, arithmetic and copies ran while one was open for 7% of the time, Pallas kernels for 0%

commit v1 on v0

--- a/solution.py
+++ b/solution.py
@@ -8,7 +8,7 @@
 
 def from_root(block, axis, holder):
     block = jnp.where(lax.axis_index(axis) == holder, block, jnp.zeros_like(block))
-    return lax.psum(block, axis)
+    return jnp.sum(lax.all_gather(block, axis), axis=0)
 
 
 def body(covariance, telemetry, active, panel):

time: 833 us -> 1730 us (2.08)
  waiting for transfers between devices: 515 us -> 1320 us
  other arithmetic: 82.5 us -> 160 us
    all_gather x0 -> x5, waiting for transfers between devices: none -> 1240 us  [from_root(): return jnp.sum(lax.all_gather(block, axis), axis=0)]
    psum x4 -> x0, waiting for transfers between devices: 426 us -> none  [from_root(): return lax.psum(block, axis)]
    reduce_sum x0 -> x5, other arithmetic: none -> 76.7 us  [from_root(): return jnp.sum(lax.all_gather(block, axis), axis=0)]
    unnamed x7 -> x9, local copies, waits for them, and re-layouts: 49.6 us -> 52.5 us
  transfers between devices with their start and end apart: 5 -> 6, of which waited for: 5 -> 6; matrix products, arithmetic and copies ran while one was open for 7% -> 5% of each run, Pallas kernels for 0% -> 0%
where the time goes in v1:
time: 1730 us; the launch traced here: 1720 us
  waiting for transfers between devices  1320 us (76%)
  other arithmetic  160 us (9%)
  local copies, waits for them, and re-layouts  114 us (7%)
  matrix products  107 us (6%)
    all_gather x5, waiting for transfers between devices, from_root(): return jnp.sum(lax.all_gather(block, axis), axis=0)  1240 us
    all_gather x1, waiting for transfers between devices, body(): column_data = lax.all_gather(local, 'row', axis=0, tiled=True)  87.7 us
    reduce_sum x5, other arithmetic, from_root(): return jnp.sum(lax.all_gather(block, axis), axis=0)  76.7 us
    dot_general x1, matrix products, body(): jnp.einsum('sat,sbu->abtu', row_data, column_data, preferred_element_type...  56.8 us
    unnamed x9, local copies, waits for them, and re-layouts  52.5 us
    broadcast_in_dim x1, local copies, waits for them, and re-layouts, body(): return result[:, None, :, None]  52.2 us
    dot_general x1, matrix products, body(): jnp.einsum('atv,buv->abtu', panel_rows, panel_cols, precision=lax.Precisi...  35.7 us
  transfers between devices with their start and end apart: 6, of which 6 were waited for; matrix products, arithmetic and copies ran while one was open for 5% of the time, Pallas kernels for 0%

profile of v1, /device:TPU:0, one launch (start us, length us, event | category | flops | bytes accessed | tf_op | source)
XLA Modules:
  0.0 1721.3 jit_solution(10017089712909365451)
XLA Ops:
  7.3 87.7 %all-gather.14.cloned.1.call-done = bf16[1536,10,1,256]{3,0,2,1:T(8,128)(2,1)} async-done(((bf16[384,10,1,256]{3,0,2,1:T(8,128)(2,1)}), bf16[1536,10,1,256]{3,0,2,1:T(8,128)(2,1)}) %all-gather.14.cloned.1.call-update) | async-done | bytes 7864336 | tf_op jit(solution)/shard_map/all_gather | solution.py:34
  95.0 9.7 bitcast_select_fusion.1
  106.5 52.4 %copy.25 = f32[20,1,10,1,256,256]{4,5,0,2,3,1:T(8,128)} copy(f32[20,1,10,1,256,256]{5,4,3,2,1,0:T(8,128)} %param.4) | data formatting | bytes 104857600 | tf_op args[0]
  160.3 474.3 %all-gather.16.cloned.1.call-done = bf16[12288,10,256]{2,0,1:T(8,128)(2,1)} async-done(((bf16[1536,10,256]{2,0,1:T(8,128)(2,1)}), bf16[12288,10,256]{2,0,1:T(8,128)(2,1)}) %all-gather.16.cloned.1.call-update) | async-done | bytes 62914576 | tf_op jit(solution)/shard_map/all_gather | solution.py:11
  634.5 34.8 %reduce_sum.57 = bf16[1536,10,256]{2,0,1:T(8,128)(2,1)} reduce(bf16[8,1536,10,256]{3,1,0,2:T(8,128)(2,1)} %bitcast.115, bf16[]{:T(256)} %constant.166.clone.1), dimensions={0}, to_apply=%region_0.1 | reduce | flops 27525120 | bytes 70778880 | tf_op jit(solution)/shard_map/reduce_sum | solution.py:11
  669.4 494.6 %all-gather.18.cloned.1.call-done = bf16[12288,10,256]{2,0,1:T(8,128)(2,1)} async-done(((bf16[1536,10,256]{2,0,1:T(8,128)(2,1)}), bf16[12288,10,256]{2,0,1:T(8,128)(2,1)}) %all-gather.18.cloned.1.call-update) | async-done | bytes 62914576 | tf_op jit(solution)/shard_map/all_gather | solution.py:11
  1164.0 24.4 %reduce_sum.58 = bf16[1536,10,256]{2,0,1:T(8,128)(2,1)} reduce(bf16[8,1536,10,256]{3,1,0,2:T(8,128)(2,1)} %bitcast.116, bf16[]{:T(256)} %constant.166.clone.1), dimensions={0}, to_apply=%region_1.2 | reduce | flops 27525120 | bytes 70778880 | tf_op jit(solution)/shard_map/reduce_sum | solution.py:11
  1188.4 7.8 pad_maximum_fusion
  1196.1 6.5 bitcast_multiply_fusion.1
  1202.7 56.8 %fusion.3 = f32[20,10,256,256]{2,3,0,1:T(8,128)} fusion(f32[20,1,10,1,256,256]{4,5,0,2,3,1:T(8,128)} %copy.25, pred[20,10]{0,1:T(8,128)(4,1)S(1)} %get-tuple-element.32, bf16[1536,20,256]{2,0,1:T(8,128)(2,1)} %bitcast_multiply_fusion.1, bf16[1536,10,1,256]{3,0,2,1:T(8,128)(2,1)} %all-gather.14.cloned.1.call-done, bf16[10,256]{1,0:T(8,128)(2,1)S(1)} %bitcast.124), kind=kOutput, calls=%fused_computation.7 | convolution fusion | flops 40333475840 | bytes 128455880 | tf_op jit(solution)/shard_map/sat,sbu->abtu/dot_general | solution.py:44
  1261.6 11.7 cholesky.51
  1273.3 9.8 custom-call.14
  1283.6 11.7 cholesky.107
  1297.3 5.0 while.1
  1302.3 20.7 %custom-call.15 = f32[2,128,128]{1,2,0:T(8,128)S(1)} custom-call(f32[2,128,128]{2,1,0:T(8,128)} %get-tuple-element.12), custom_call_target="InvertDiagBlocksLowerTriangular" | custom-call | tf_op jit(solution)/shard_map/triangular_solve | solution.py:53
  1324.7 24.8 %all-gather.12.cloned.1.call-done = f32[4,256,256]{2,1,0:T(8,128)} async-done(((f32[1,256,256]{2,1,0:T(8,128)}), f32[4,256,256]{2,1,0:T(8,128)}) %all-gather.12.cloned.1.call-update) | async-done | bytes 1048592 | tf_op jit(solution)/shard_map/all_gather | solution.py:11
  1350.8 12.9 fusion.10
  1364.1 185.3 %all-gather.20.cloned.1.call-done = bf16[160,256,256]{2,1,0:T(8,128)(2,1)} async-done(((bf16[20,256,256]{2,1,0:T(8,128)(2,1)}), bf16[160,256,256]{2,1,0:T(8,128)(2,1)}) %all-gather.20.cloned.1.call-update) | async-done | bytes 20971536 | tf_op jit(solution)/shard_map/all_gather | solution.py:11
  1549.3 11.3 reduce_sum.60
  1562.1 3.2 copy.30
  1565.3 56.2 %all-gather.22.cloned.1.call-done = bf16[40,1,256,256]{3,2,1,0:T(8,128)(2,1)} async-done(((bf16[10,1,256,256]{3,2,1,0:T(8,128)(2,1)}), bf16[40,1,256,256]{3,2,1,0:T(8,128)(2,1)}) %all-gather.22.cloned.1.call-update) | async-done | bytes 5242896 | tf_op jit(solution)/shard_map/all_gather | solution.py:11
  1621.5 4.8 bitcast_reduce_fusion
  1626.3 35.7 %fusion.2 = f32[20,1,10,1,256,256]{4,5,0,2,3,1:T(8,128)} fusion(f32[20,10,256,256]{2,3,0,1:T(8,128)} %fusion.3, f32[20,256,256]{1,2,0:T(8,128)} %copy.30, f32[256,256]{0,1:T(8,128)S(1)} %copy.28, pred[20,10]{0,1:T(8,128)(4,1)S(1)} %copy-done.1, pred[20,10]{0,1:T(8,128)(4,1)S(1)} %get-tuple-element.34, pred[20,10]{0,1:T(8,128)(4,1)S(1)} %get-tuple-element.33, ...), kind=kOutput, calls=%fused_computation.5 | convolution fusion | flops 6763315200 | bytes 114295384 | tf_op jit(solution)/shard_map/atv,buv->abtu/dot_general | solution.py:75
  1662.0 52.2 %copy.31 = f32[20,1,10,1,256,256]{5,4,3,2,1,0:T(8,128)} copy(f32[20,1,10,1,256,256]{4,5,0,2,3,1:T(8,128)} %fusion.2) | data formatting | bytes 104857600 | tf_op jit(solution)/shard_map/broadcast_in_dim | solution.py:87
  (61 shorter events, 16.1 us)
Async XLA Ops:
  6.5 88.5 %all-gather.14.cloned.1.call-start = ((), (), s32[]{:S(2)}) async-start(), calls=%async_computation.1 | async-start | bytes 9830400 | tf_op jit(solution)/shard_map/all_gather | solution.py:34
  7.3 627.3 %all-gather.16.cloned.1.call-start = ((), (), s32[]{:S(2)}) async-start(), calls=%async_computation.2 | async-start | bytes 70778880 | tf_op jit(solution)/shard_map/all_gather | solution.py:11
  104.8 1.5 copy-start.2
  104.8 1059.2 %all-gather.18.cloned.1.call-start = ((), (), s32[]{:S(2)}) async-start(), calls=%async_computation.3 | async-start | bytes 70778880 | tf_op jit(solution)/shard_map/all_gather | solution.py:11
  105.5 1243.9 %all-gather.12.cloned.1.call-start = ((), (), s32[]{:S(2)}) async-start(), calls=%async_computation | async-start | bytes 1310720 | tf_op jit(solution)/shard_map/all_gather | solution.py:11
  1202.7 120.4 %copy-start = (pred[256,256]{1,0:T(32,128)(4,1)S(1)}, pred[256,256]{1,0:T(32,128)(4,1)}, u32[]{:S(2)}) copy-start(pred[256,256]{1,0:T(32,128)(4,1)} %iota_compare_fusion) | copy-start | bytes 196612
  1324.6 224.7 %all-gather.20.cloned.1.call-start = ((), (), s32[]{:S(2)}) async-start(), calls=%async_computation.4 | async-start | bytes 23592960 | tf_op jit(solution)/shard_map/all_gather | solution.py:11
  1363.7 257.8 %all-gather.22.cloned.1.call-start = ((), (), s32[]{:S(2)}) async-start(), calls=%async_computation.5 | async-start | bytes 6553600 | tf_op jit(solution)/shard_map/all_gather | solution.py:11
  1561.9 64.4 %copy-start.1 = (pred[20,10]{0,1:T(8,128)(4,1)S(1)}, pred[20,10]{0,1:T(8,128)(4,1)}, u32[]{:S(2)}) copy-start(pred[20,10]{0,1:T(8,128)(4,1)} %get-tuple-element.31) | copy-start | bytes 604
Sparse Core Ops, SparseCore 0:
  9.2 85.8 all-gather.13
  104.9 529.5 all-gather.15
  636.2 527.7 all-gather.17
  1324.8 24.6 all-gather.11
  1363.9 185.4 all-gather.19
  1562.0 59.4 all-gather.21
